TPU v7x, 256 devices: a whole 4x4x8 slice. The times are simulated.
256 devices in a mesh: gx: 16 (over y, x), gy: 16 (over z, core).
Axes of the slice: x: 4, y: 4, z: 8, core: 2. Of those that a mesh axis runs over, the one named last changes fastest.
Arguments:
- energy: float32 [256, 2048, 128], P('gx', 'gy'), may hold values from 1 to 5
- coupling: float32 [256, 2048, 128], P('gx', 'gy'), may hold values from 4000 to 40000
Outputs:
- energy_next: float32 [256, 2048, 128], P('gx', 'gy')
All inputs are finite; a program needn't handle non-finite values.
Results may differ from a plain program's by a relative error of at most 0.0003.
Values sent between devices are 32-bit elements; how exact they have to be, the bound alone decides.
No kernel may reach another device: no remote copies, remote signals or barrier semaphores. Data moves between devices by JAX's collectives and lax.ppermute only.
A program may use at most 64 MiB of HBM per device.

v0:
```python
import jax
import jax.numpy as jnp
from jax import lax
from jax.sharding import PartitionSpec as P

y_weight = 0.15


def with_halo(shard, sides, width):
    for axis, dim in sides:
        size, length = (lax.axis_size(axis), shard.shape[dim])
        up = [(i, (i + 1) % size) for i in range(size - 1)]
        down = [(j, i) for i, j in up]
        last = lax.slice_in_dim(shard, length - width, length, axis=dim)
        initial = lax.slice_in_dim(shard, 0, width, axis=dim)
        before = lax.ppermute(last, axis, up)
        after = lax.ppermute(initial, axis, down)
        shard = jnp.concatenate([before, shard, after], axis=dim)
    return shard


def shifted(value, axis, steps):
    count = lax.axis_size(axis)
    initial, last = (max(0, -steps), min(count, count - steps))
    return lax.ppermute(value, axis, [(source, source + steps) for source in range(initial, last)])


def many_solve(diag_part, lower_part, upper_part, sources):

    def forward(running, row):
        prev_ratio, prev_value = running
        diag_row, lower_row, upper_row, source_row = row
        denom = diag_row - lower_row * prev_ratio
        new_ratio = upper_row / denom
        new_value = (source_row - lower_row[None] * prev_value) / denom[None]
        return ((new_ratio, new_value), (new_ratio, new_value))

    start = (jnp.zeros(diag_part.shape[1:], jnp.float32), jnp.zeros(sources.shape[1:], jnp.float32))
    _, (ratios, values) = lax.scan(forward, start, (diag_part, lower_part, upper_part, sources))

    def backward(later_value, row):
        ratio_row, value_row = row
        result = value_row - ratio_row[None] * later_value
        return (result, result)

    _, solved = lax.scan(
        backward, jnp.zeros(sources.shape[1:], jnp.float32), (ratios, values), reverse=True
    )
    return solved


def body(energy, coupling):
    padded = with_halo(energy, (("gy", 1),), 1)
    source_term = energy + y_weight * (padded[:, :-2] - 2.0 * energy + padded[:, 2:])
    height = energy.shape[0]
    inner_diag = 1.0 + coupling[: height - 1] + coupling[1:height]
    inner_lower = -coupling[: height - 1]
    inner_upper = -coupling[1:height]
    blank = jnp.zeros_like(coupling[: height - 1])
    left_source = jnp.concatenate([coupling[:1], blank[1:]], 0)
    right_source = jnp.concatenate([blank[1:], coupling[height - 1 : height]], 0)
    sources = jnp.stack([source_term[: height - 1], left_source, right_source], 1)
    solved = many_solve(inner_diag, inner_lower, inner_upper, sources)
    local_part = solved[:, 0]
    left_reply = solved[:, 1]
    right_reply = solved[:, 2]
    first_rows = jnp.stack([local_part[0], left_reply[0], right_reply[0], coupling[0]], 0)
    following = shifted(first_rows, "gx", -1)
    next_local = following[0]
    next_left = following[1]
    next_right = following[2]
    next_face = following[3]
    own_face = coupling[height - 1]
    position = lax.axis_index("gx")
    lower_coef = jnp.where(position == 0, 0.0, -own_face * left_reply[height - 2])
    middle = 1.0 + own_face + next_face - own_face * right_reply[height - 2] - next_face * next_left
    upper_coef = -next_face * next_right
    target = source_term[height - 1] + own_face * local_part[height - 2] + next_face * next_local
    bundle = jnp.stack([lower_coef, middle, upper_coef, target], 0)[None]
    gathered = lax.all_gather(bundle, "gx", axis=0, tiled=True)
    whole = many_solve(gathered[:, 1], gathered[:, 0], gathered[:, 2], gathered[:, 3][:, None])
    last_value = lax.dynamic_index_in_dim(whole[:, 0], position, 0, keepdims=False)
    previous = shifted(last_value, "gx", 1)
    interior = local_part + left_reply * previous[None] + right_reply * last_value[None]
    return jnp.concatenate([interior, last_value[None]], 0)


def solution(mesh):
    in_specs = (P("gx", "gy", None), P("gx", "gy", None))
    out_specs = P("gx", "gy", None)
    return jax.shard_map(body, mesh=mesh, in_specs=in_specs, out_specs=out_specs, check_vma=False)
```

profile of v0, /device:TPU:8, one launch (start us, length us, event | category | flops | bytes accessed | tf_op | source)
XLA Modules:
  0.0 257.6 jit_solution(15537490057633315321)
XLA Ops:
  7.4 1.7 collective-permute-start
  11.4 3.7 %select_bitcast_fusion = (f32[15,1,128,128]{3,2,0,1:T(8,128)}, f32[15,128,128]{2,1,0:T(8,128)}, f32[15,128,128]{2,1,0:T(8,128)}, f32[15,128,128]{2,1,0:T(8,128)}) fusion(f32[16,128,128]{2,1,0:T(8,128)} %param.11, pred[15]{0:T(512)(128)(4,1)} %constant.130.clone.1), kind=kLoop, calls=%fused_computation.44 | loop fusion | flops 1228800 | bytes 5898255 | tf_op jit(solution)/shard_map/stack | solution.py:62
  18.2 1.9 broadcast.28.clone
  21.2 34.4 %while.68 = (s32[]{:T(128)}, f32[128,128]{1,0:T(8,128)S(1)}, f32[3,128,128]{2,1,0:T(8,128)S(1)}, f32[15,128,128]{2,1,0:T(8,128)}, f32[15,3,128,128]{3,2,1,0:T(8,...) while((s32[]{:T(128)}, f32[128,128]{1,0:T(8,128)S(1)}, ...), condition=%wide.region_1.2_spmd.clone, body=%wide.region_0.1_spmd.clone.sunk | while | flops 262147 | bytes 1442936 | solution.py:39
  21.2 1.5 bitcast_dynamic-update-slice_fusion.12
  23.5 1.5 bitcast_dynamic-update-slice_fusion.12
  25.8 1.5 bitcast_dynamic-update-slice_fusion.12
  30.4 1.5 bitcast_dynamic-update-slice_fusion.12
  32.7 1.5 bitcast_dynamic-update-slice_fusion.12
  35.0 1.5 bitcast_dynamic-update-slice_fusion.12
  37.3 1.5 bitcast_dynamic-update-slice_fusion.12
  39.6 1.5 bitcast_dynamic-update-slice_fusion.12
  41.9 1.5 bitcast_dynamic-update-slice_fusion.12
  44.2 1.5 bitcast_dynamic-update-slice_fusion.12
  48.7 1.5 bitcast_dynamic-update-slice_fusion.12
  51.0 1.5 bitcast_dynamic-update-slice_fusion.12
  53.3 1.5 bitcast_dynamic-update-slice_fusion.12
  55.9 28.5 %while.69 = (s32[]{:T(128)}, f32[3,128,128]{2,1,0:T(8,128)S(1)}, f32[15,3,128,128]{3,2,1,0:T(8,128)S(1)}, f32[15,3,128,128]{3,2,1,0:T(8,128)}, f32[15,128,128]{2...) while((s32[]{:T(128)}, f32[3,128,128]{2,1,0:T(8,128)S(1)}, f32[15,3,128,128]{3,2,1,0:T(8,128)S(1)}, ...), condition=%wide.region_3.4_spmd.clone, body=%wide.region_2.3_spmd.clone.sunk | while | flops 147460 | bytes 983155 | solution.py:46
  84.5 4.6 %collective-permute-start.2 = (f32[4,128,128]{2,1,0:T(8,128)S(1)}, f32[4,128,128]{2,1,0:T(8,128)S(1)}, u32[]{:S(2)}, u32[]{:S(2)}) collective-permute-start(f32[4,128,128]{2,1,0:T(8,128)S(1)} %pad_maximum_fusion.4), channel_id=1, source_target_pairs={{16,0},{32,16},{48,32},{64,48},{80,64},{96,80},{112,96},{128,112},... | collective-permute-start | bytes 786440 | tf_op jit(solution)/shard_map/ppermute | solution.py:25
  89.1 4.8 %collective-permute-done.2 = f32[4,128,128]{2,1,0:T(8,128)S(1)} collective-permute-done((f32[4,128,128]{2,1,0:T(8,128)S(1)}, f32[4,128,128]{2,1,0:T(8,128)S(1)}, u32[]{:S(2)}, u32[]{:S(2)}) %collective-permute-start.2) | collective-permute-done | bytes 262176 | tf_op jit(solution)/shard_map/ppermute | solution.py:25
  95.6 63.9 %all-gather.3.cloned.1.call-done = f32[64,128,128]{2,1,0:T(8,128)} async-done(((f32[4,128,128]{2,1,0:T(8,128)}), f32[64,128,128]{2,1,0:T(8,128)}) %all-gather.3.cloned.1.call-update) | async-done | bytes 4194320 | tf_op jit(solution)/shard_map/all_gather | solution.py:80
  159.5 4.3 %fusion.15 = (f32[16,1,128,128]{3,2,1,0:T(8,128)}, f32[16,128,128]{2,1,0:T(8,128)}, f32[16,128,128]{2,1,0:T(8,128)}, f32[16,128,128]{2,1,0:T(8,128)}) fusion(f32[16,4,128,128]{3,2,1,0:T(8,128)} %bitcast.136), kind=kLoop, calls=%fused_computation.66 | loop fusion | bytes 8388608 | tf_op jit(solution)/shard_map/slice | solution.py:81
  164.9 49.7 %while.70 = (s32[]{:T(128)}, f32[128,128]{1,0:T(8,128)S(1)}, f32[1,128,128]{2,1,0:T(8,128)S(1)}, f32[16,128,128]{2,1,0:T(8,128)}, f32[16,1,128,128]{3,2,1,0:T(8,...) while((s32[]{:T(128)}, f32[128,128]{1,0:T(8,128)S(1)}, ...), condition=%wide.region_5.6_spmd.clone, body=%wide.region_4.5_spmd.clone.sunk | while | flops 180227 | bytes 854135 | solution.py:39
  164.9 1.6 bitcast_dynamic-update-slice_fusion.16
  166.5 1.5 bitcast_dynamic-update-slice_fusion.15
  168.0 1.6 bitcast_dynamic-update-slice_fusion.16
  169.6 1.5 bitcast_dynamic-update-slice_fusion.15
  171.1 1.6 bitcast_dynamic-update-slice_fusion.16
  172.7 1.5 bitcast_dynamic-update-slice_fusion.15
  174.2 1.6 bitcast_dynamic-update-slice_fusion.16
  175.8 1.5 bitcast_dynamic-update-slice_fusion.15
  177.3 1.6 bitcast_dynamic-update-slice_fusion.16
  178.9 1.5 bitcast_dynamic-update-slice_fusion.15
  180.4 1.6 bitcast_dynamic-update-slice_fusion.16
  182.0 1.6 bitcast_dynamic-update-slice_fusion.15
  183.5 1.6 bitcast_dynamic-update-slice_fusion.16
  186.6 1.6 bitcast_dynamic-update-slice_fusion.16
  188.2 1.5 bitcast_dynamic-update-slice_fusion.15
  189.7 1.6 bitcast_dynamic-update-slice_fusion.16
  191.3 1.6 bitcast_dynamic-update-slice_fusion.15
  192.9 1.6 bitcast_dynamic-update-slice_fusion.16
  194.4 1.6 bitcast_dynamic-update-slice_fusion.15
  196.0 1.6 bitcast_dynamic-update-slice_fusion.16
  197.6 1.5 bitcast_dynamic-update-slice_fusion.15
  199.1 1.6 bitcast_dynamic-update-slice_fusion.16
  200.7 1.5 bitcast_dynamic-update-slice_fusion.15
  202.2 1.6 bitcast_dynamic-update-slice_fusion.16
  203.8 1.5 bitcast_dynamic-update-slice_fusion.15
  205.3 1.6 bitcast_dynamic-update-slice_fusion.16
  208.4 1.6 bitcast_dynamic-update-slice_fusion.16
  210.0 1.5 bitcast_dynamic-update-slice_fusion.15
  211.5 1.6 bitcast_dynamic-update-slice_fusion.16
  213.1 1.5 bitcast_dynamic-update-slice_fusion.15
  215.7 24.7 %while.71 = (s32[]{:T(128)}, f32[1,128,128]{2,1,0:T(8,128)S(1)}, f32[16,1,128,128]{3,2,1,0:T(8,128)}, f32[16,1,128,128]{3,2,1,0:T(8,128)}, f32[16,128,128]{2,1,0:T(8,128)}, /*index=5*/s32[]{:T(128)}, s32[]{:T(128)}, s32[]{:T(128)}) while((s32[]{:T(128)}, f32[1,128,128]{2,1,0:T(8,128)S(1)}, f32[16,1,128,128]{3,2,1,0:T(8,128)}, ...), condition=%wide.region_7.8_spmd.clone, body=%wide.region_6.7_spmd.clone.sunk | while | flops 49156 | bytes 327791 | solution.py:46
  215.7 1.5 bitcast_dynamic-update-slice_fusion.17
  217.2 1.5 bitcast_dynamic-update-slice_fusion.17
  218.8 1.5 bitcast_dynamic-update-slice_fusion.17
  220.3 1.5 bitcast_dynamic-update-slice_fusion.17
  221.9 1.5 bitcast_dynamic-update-slice_fusion.17
  223.4 1.5 bitcast_dynamic-update-slice_fusion.17
  225.0 1.5 bitcast_dynamic-update-slice_fusion.17
  228.0 1.5 bitcast_dynamic-update-slice_fusion.17
  241.2 2.2 collective-permute-start.3
  243.4 6.1 %collective-permute-done.3 = f32[128,128]{1,0:T(8,128)S(1)} collective-permute-done((f32[128,128]{1,0:T(8,128)S(1)}, f32[128,128]{1,0:T(8,128)S(1)}, u32[]{:S(2)}, u32[]{:S(2)}) %collective-permute-start.3) | collective-permute-done | bytes 65568 | tf_op jit(solution)/shard_map/ppermute | solution.py:25
  (94 shorter events, 71.5 us)
Async XLA Ops:
  6.5 153.0 %all-gather.3.cloned.1.call-start = ((), (), s32[]{:S(2)}) async-start(), calls=%async_computation | async-start | bytes 4456448 | tf_op jit(solution)/shard_map/all_gather | solution.py:80
  7.4 8.7 %collective-permute-start = (f32[16,1,128]{2,1,0:T(1,128)S(1)}, f32[16,1,128]{2,1,0:T(1,128)S(1)}, u32[]{:S(2)}, u32[]{:S(2)}) collective-permute-start(f32[16,1,128]{2,1,0:T(1,128)S(1)} %get-tuple-element.509), channel_id=1, source_target_pairs={{0,1},{1,2},{2,3},{3,4},{4,5},{5,6},{6,7},{7,8},{8,9},{9,10},{10,1... | collective-permute-start | bytes 24584 | tf_op jit(solution)/shard_map/ppermute | solution.py:16
  9.2 7.0 %collective-permute-start.1 = (f32[16,1,128]{2,1,0:T(1,128)S(1)}, f32[16,1,128]{2,1,0:T(1,128)S(1)}, u32[]{:S(2)}, u32[]{:S(2)}) collective-permute-start(f32[16,1,128]{2,1,0:T(1,128)S(1)} %get-tuple-element.510), channel_id=1, source_target_pairs={{1,0},{2,1},{3,2},{4,3},{5,4},{6,5},{7,6},{8,7},{9,8},{10,9},{11,1... | collective-permute-start | bytes 24584 | tf_op jit(solution)/shard_map/ppermute | solution.py:17
  11.4 4.8 %copy-start.3 = (f32[16,128,128]{2,1,0:T(8,128)S(1)}, f32[16,128,128]{2,1,0:T(8,128)}, u32[]{:S(2)}) copy-start(f32[16,128,128]{2,1,0:T(8,128)} %param.10) | copy-start | bytes 3145732
  16.2 1.3 copy-start.1
  16.2 1.9 copy-start.2
  16.5 1.0 copy-start
  84.5 9.4 %collective-permute-start.2 = (f32[4,128,128]{2,1,0:T(8,128)S(1)}, f32[4,128,128]{2,1,0:T(8,128)S(1)}, u32[]{:S(2)}, u32[]{:S(2)}) collective-permute-start(f32[4,128,128]{2,1,0:T(8,128)S(1)} %pad_maximum_fusion.4), channel_id=1, source_target_pairs={{16,0},{32,16},{48,32},{64,48},{80,64},{96,80},{112,96},{128,112},... | collective-permute-start | bytes 786440 | tf_op jit(solution)/shard_map/ppermute | solution.py:25
  241.2 8.3 %collective-permute-start.3 = (f32[128,128]{1,0:T(8,128)S(1)}, f32[128,128]{1,0:T(8,128)S(1)}, u32[]{:S(2)}, u32[]{:S(2)}) collective-permute-start(f32[128,128]{1,0:T(8,128)S(1)} %get-tuple-element.507), channel_id=1, source_target_pairs={{0,16},{16,32},{32,48},{48,64},{64,80},{80,96},{96,112},{112,128},... | collective-permute-start | bytes 196616 | tf_op jit(solution)/shard_map/ppermute | solution.py:25
Sparse Core Ops, SparseCore 0:
  95.7 63.7 all-gather.2
where the time goes:
time: 262 us; the launch traced here: 258 us
  other arithmetic  131 us (50%)
  waiting for transfers between devices  74.8 us (29%)
  local copies, waits for them, and re-layouts  27.8 us (11%)
  between operations  13.6 us (5%)
  starting transfers between devices  9.76 us (4%)
    dynamic_update_slice x93, other arithmetic, many_solve(): lax.scan(forward, start, (diag_part, lower_part, upper_part, sources))  124 us
    all_gather x1, waiting for transfers between devices, body(): gathered = lax.all_gather(bundle, 'gx', axis=0, tiled=True)  63.9 us
    mul x15, local copies, waits for them, and re-layouts, backward(): result = value_row - ratio_row[None] * later_value  12.7 us
    ppermute x2, waiting for transfers between devices, shifted(): lax.ppermute(value, axis, [(source, source + steps) for source in range(i...  10.9 us
    ppermute x2, starting transfers between devices, shifted(): lax.ppermute(value, axis, [(source, source + steps) for source in range(i...  6.73 us
  transfers between devices with their start and end apart: 5, of which 3 were waited for; matrix products, arithmetic and copies ran while one was open for 2% of the time, Pallas kernels for 0%

commit v1 on v0

--- a/solution.py
+++ b/solution.py
@@ -4,6 +4,28 @@
 from jax.sharding import PartitionSpec as P
 
 y_weight = 0.15
+
+
+def in_order(pieces, dim):
+    shape = list(pieces.shape[1:])
+    shape[dim] *= pieces.shape[0]
+    return jnp.moveaxis(pieces, 0, dim).reshape(shape)
+
+
+def ring_gather(x, axis, dim):
+    count = lax.axis_size(axis)
+    pairs = [(i, (i + 1) % count) for i in range(count)]
+    back = [(b, a) for a, b in pairs]
+    lower, upper = ([], [])
+    for step in range(count - 1):
+        if step % 2 == 0:
+            lower.append(lax.ppermute(lower[-1] if lower else x, axis, pairs))
+        else:
+            upper.append(lax.ppermute(upper[-1] if upper else x, axis, back))
+    blocks = jnp.stack([*lower[::-1], x, *upper])
+    shift = lax.axis_index(axis) - len(lower)
+    blocks = blocks[(jnp.arange(count) - shift) % count]
+    return in_order(blocks, dim)
 
 
 def with_halo(shard, sides, width):
@@ -77,7 +99,7 @@
     upper_coef = -next_face * next_right
     target = source_term[height - 1] + own_face * local_part[height - 2] + next_face * next_local
     bundle = jnp.stack([lower_coef, middle, upper_coef, target], 0)[None]
-    gathered = lax.all_gather(bundle, "gx", axis=0, tiled=True)
+    gathered = ring_gather(bundle, "gx", 0)
     whole = many_solve(gathered[:, 1], gathered[:, 0], gathered[:, 2], gathered[:, 3][:, None])
     last_value = lax.dynamic_index_in_dim(whole[:, 0], position, 0, keepdims=False)
     previous = shifted(last_value, "gx", 1)

time: 262 us -> 296 us (1.13)
  the two profiles are of different devices: /device:TPU:8 before, /device:TPU:130 now
where the time goes in v1:
time: 296 us; the launch traced here: 291 us
  other arithmetic  132 us (45%)
  local copies, waits for them, and re-layouts  55.4 us (19%)
  waiting for transfers between devices  53.3 us (18%)
  starting transfers between devices  49.7 us (17%)
    dynamic_update_slice x93, other arithmetic, many_solve(): lax.scan(forward, start, (diag_part, lower_part, upper_part, sources))  124 us
    ppermute x8, waiting for transfers between devices, ring_gather(): lower.append(lax.ppermute(lower[-1] if lower else x, axis, pairs))  38.1 us
    ppermute x7, starting transfers between devices, ring_gather(): upper.append(lax.ppermute(upper[-1] if upper else x, axis, back))  28.3 us
    unnamed x50, local copies, waits for them, and re-layouts  23.2 us
    ppermute x2, waiting for transfers between devices, shifted(): lax.ppermute(value, axis, [(source, source + steps) for source in range(i...  12.9 us
    mul x15, local copies, waits for them, and re-layouts, backward(): result = value_row - ratio_row[None] * later_value  12.7 us
    ppermute x8, starting transfers between devices, ring_gather(): lower.append(lax.ppermute(lower[-1] if lower else x, axis, pairs))  10.2 us
  transfers between devices with their start and end apart: 19, of which 14 were waited for; matrix products, arithmetic and copies ran while one was open for 9% of the time, Pallas kernels for 0%

profile of v1, /device:TPU:130, one launch (start us, length us, event | category | flops | bytes accessed | tf_op | source)
XLA Modules:
  0.0 290.6 jit_solution(3794068992273049484)
XLA Ops:
  1.0 1.9 collective-permute-start
  2.9 4.9 %collective-permute-start.1 = (f32[16,1,128]{2,1,0:T(1,128)S(1)}, f32[16,1,128]{2,1,0:T(1,128)S(1)}, u32[]{:S(2)}, u32[]{:S(2)}) collective-permute-start(f32[16,1,128]{2,1,0:T(1,128)S(1)} %get-tuple-element.501), channel_id=1, source_target_pairs={{1,0},{2,1},{3,2},{4,3},{5,4},{6,5},{7,6},{8,7},{9,8},{10,9},{11,1... | collective-permute-start | bytes 24584 | tf_op jit(solution)/shard_map/ppermute | solution.py:39
  8.7 3.7 %select_bitcast_fusion = (f32[15,1,128,128]{3,2,0,1:T(8,128)}, f32[15,128,128]{2,1,0:T(8,128)}, f32[15,128,128]{2,1,0:T(8,128)}, f32[15,128,128]{2,1,0:T(8,128)}) fusion(f32[16,128,128]{2,1,0:T(8,128)} %param.11, pred[15]{0:T(512)(128)(4,1)} %constant.146.clone.1), kind=kLoop, calls=%fused_computation.45 | loop fusion | flops 1228800 | bytes 5898255 | tf_op jit(solution)/shard_map/stack | solution.py:84
  15.5 1.9 broadcast.91.clone
  18.5 34.4 %while.68 = (s32[]{:T(128)}, f32[128,128]{1,0:T(8,128)S(1)}, f32[3,128,128]{2,1,0:T(8,128)S(1)}, f32[15,128,128]{2,1,0:T(8,128)}, f32[15,3,128,128]{3,2,1,0:T(8,...) while((s32[]{:T(128)}, f32[128,128]{1,0:T(8,128)S(1)}, ...), condition=%wide.region_1.2_spmd.clone, body=%wide.region_0.1_spmd.clone.sunk | while | flops 262147 | bytes 1442936 | solution.py:61
  20.7 1.6 bitcast_dynamic-update-slice_fusion.28
  23.0 1.6 bitcast_dynamic-update-slice_fusion.28
  25.4 1.6 bitcast_dynamic-update-slice_fusion.28
  36.8 1.6 bitcast_dynamic-update-slice_fusion.28
  53.2 28.5 %while.69 = (s32[]{:T(128)}, f32[3,128,128]{2,1,0:T(8,128)S(1)}, f32[15,3,128,128]{3,2,1,0:T(8,128)S(1)}, f32[15,3,128,128]{3,2,1,0:T(8,128)}, f32[15,128,128]{2...) while((s32[]{:T(128)}, f32[3,128,128]{2,1,0:T(8,128)S(1)}, f32[15,3,128,128]{3,2,1,0:T(8,128)S(1)}, ...), condition=%wide.region_3.4_spmd.clone, body=%wide.region_2.3_spmd.clone.sunk | while | flops 147460 | bytes 983155 | solution.py:68
  81.8 2.4 collective-permute-start.2
  84.2 5.9 %collective-permute-done.2 = f32[4,128,128]{2,1,0:T(8,128)} collective-permute-done((f32[4,128,128]{2,1,0:T(8,128)S(1)}, f32[4,128,128]{2,1,0:T(8,128)}, u32[]{:S(2)}, u32[]{:S(2)}) %collective-permute-start.2) | collective-permute-done | bytes 262176 | tf_op jit(solution)/shard_map/ppermute | solution.py:47
  91.3 1.6 collective-permute-start.3
  92.8 4.9 %collective-permute-done.3 = f32[1,4,128,128]{3,2,1,0:T(8,128)S(1)} collective-permute-done((f32[1,4,128,128]{3,2,1,0:T(8,128)S(1)}, f32[1,4,128,128]{3,2,1,0:T(8,128)S(1)}, u32[]{:S(2)}, u32[]{:S(2)}) %collective-permute-start.3) | collective-permute-done | bytes 262176 | tf_op jit(solution)/shard_map/ppermute | solution.py:22
  98.4 2.8 collective-permute-start.4
  102.3 4.9 %collective-permute-done.4 = f32[1,4,128,128]{3,2,1,0:T(8,128)S(1)} collective-permute-done((f32[1,4,128,128]{3,2,1,0:T(8,128)S(1)}, f32[1,4,128,128]{3,2,1,0:T(8,128)S(1)}, u32[]{:S(2)}, u32[]{:S(2)}) %collective-permute-start.4) | collective-permute-done | bytes 262176 | tf_op jit(solution)/shard_map/ppermute | solution.py:22
  107.2 2.8 collective-permute-start.5
  110.7 2.0 collective-permute-start.12
  112.7 3.8 %collective-permute-done.5 = f32[1,4,128,128]{3,2,1,0:T(8,128)S(1)} collective-permute-done((f32[1,4,128,128]{3,2,1,0:T(8,128)S(1)}, f32[1,4,128,128]{3,2,1,0:T(8,128)S(1)}, u32[]{:S(2)}, u32[]{:S(2)}) %collective-permute-start.5) | collective-permute-done | bytes 262176 | tf_op jit(solution)/shard_map/ppermute | solution.py:22
  116.5 2.5 collective-permute-start.6
  119.5 2.9 collective-permute-start.13
  122.4 4.9 %collective-permute-done.6 = f32[1,4,128,128]{3,2,1,0:T(8,128)S(1)} collective-permute-done((f32[1,4,128,128]{3,2,1,0:T(8,128)S(1)}, f32[1,4,128,128]{3,2,1,0:T(8,128)S(1)}, u32[]{:S(2)}, u32[]{:S(2)}) %collective-permute-start.6) | collective-permute-done | bytes 262176 | tf_op jit(solution)/shard_map/ppermute | solution.py:22
  128.6 5.1 %collective-permute-start.14 = (f32[1,4,128,128]{3,2,1,0:T(8,128)S(1)}, f32[1,4,128,128]{3,2,1,0:T(8,128)S(1)}, u32[]{:S(2)}, u32[]{:S(2)}) collective-permute-start(f32[1,4,128,128]{3,2,1,0:T(8,128)S(1)} %collective-permute-done.13), channel_id=1, source_target_pairs={{16,0},{32,16},{48,32},{64,48},{80,64},{96,80},{112,96},{128,112},... | collective-permute-start | bytes 786440 | tf_op jit(solution)/shard_map/ppermute | solution.py:24
  133.7 5.7 %collective-permute-done.7 = f32[1,4,128,128]{3,2,1,0:T(8,128)S(1)} collective-permute-done((f32[1,4,128,128]{3,2,1,0:T(8,128)S(1)}, f32[1,4,128,128]{3,2,1,0:T(8,128)S(1)}, u32[]{:S(2)}, u32[]{:S(2)}) %collective-permute-start.7) | collective-permute-done | bytes 262176 | tf_op jit(solution)/shard_map/ppermute | solution.py:22
  140.2 6.0 %collective-permute-start.15 = (f32[1,4,128,128]{3,2,1,0:T(8,128)S(1)}, f32[1,4,128,128]{3,2,1,0:T(8,128)}, u32[]{:S(2)}, u32[]{:S(2)}) collective-permute-start(f32[1,4,128,128]{3,2,1,0:T(8,128)S(1)} %collective-permute-done.14), channel_id=1, source_target_pairs={{16,0},{32,16},{48,32},{64,48},{80,64},{96,80},{112,96},{128,112},... | collective-permute-start | bytes 786440 | tf_op jit(solution)/shard_map/ppermute | solution.py:24
  146.2 5.5 %collective-permute-done.8 = f32[1,4,128,128]{3,2,1,0:T(8,128)S(1)} collective-permute-done((f32[1,4,128,128]{3,2,1,0:T(8,128)S(1)}, f32[1,4,128,128]{3,2,1,0:T(8,128)S(1)}, u32[]{:S(2)}, u32[]{:S(2)}) %collective-permute-start.8) | collective-permute-done | bytes 262176 | tf_op jit(solution)/shard_map/ppermute | solution.py:22
  152.3 5.6 %collective-permute-start.16 = (f32[1,4,128,128]{3,2,1,0:T(8,128)}, f32[1,4,128,128]{3,2,1,0:T(8,128)}, u32[]{:S(2)}, u32[]{:S(2)}) collective-permute-start(f32[1,4,128,128]{3,2,1,0:T(8,128)} %collective-permute-done.15), channel_id=1, source_target_pairs={{16,0},{32,16},{48,32},{64,48},{80,64},{96,80},{112,96},{128,112},... | collective-permute-start | bytes 786440 | tf_op jit(solution)/shard_map/ppermute | solution.py:24
  157.9 4.9 %collective-permute-done.9 = f32[1,4,128,128]{3,2,1,0:T(8,128)} collective-permute-done((f32[1,4,128,128]{3,2,1,0:T(8,128)S(1)}, f32[1,4,128,128]{3,2,1,0:T(8,128)}, u32[]{:S(2)}, u32[]{:S(2)}) %collective-permute-start.9) | collective-permute-done | bytes 262176 | tf_op jit(solution)/shard_map/ppermute | solution.py:22
  163.3 5.8 %collective-permute-start.17 = (f32[1,4,128,128]{3,2,1,0:T(8,128)}, f32[1,4,128,128]{3,2,1,0:T(8,128)S(1)}, u32[]{:S(2)}, u32[]{:S(2)}) collective-permute-start(f32[1,4,128,128]{3,2,1,0:T(8,128)} %collective-permute-done.16), channel_id=1, source_target_pairs={{16,0},{32,16},{48,32},{64,48},{80,64},{96,80},{112,96},{128,112},... | collective-permute-start | bytes 786440 | tf_op jit(solution)/shard_map/ppermute | solution.py:24
  169.1 3.4 %collective-permute-done.10 = f32[1,4,128,128]{3,2,1,0:T(8,128)} collective-permute-done((f32[1,4,128,128]{3,2,1,0:T(8,128)}, f32[1,4,128,128]{3,2,1,0:T(8,128)}, u32[]{:S(2)}, u32[]{:S(2)}) %collective-permute-start.10) | collective-permute-done | bytes 262176 | tf_op jit(solution)/shard_map/ppermute | solution.py:22
  172.5 1.7 bitcast_dynamic-update-slice_fusion.21
  174.2 1.7 bitcast_dynamic-update-slice_fusion.20
  175.9 1.7 bitcast_dynamic-update-slice_fusion.19
  177.6 1.7 bitcast_dynamic-update-slice_fusion.18
  179.2 1.7 bitcast_dynamic-update-slice_fusion.17
  180.9 1.7 bitcast_dynamic-update-slice_fusion.16
  182.5 1.7 bitcast_dynamic-update-slice_fusion.15
  184.2 1.7 bitcast_dynamic-update-slice_fusion.14
  189.5 1.7 bitcast_dynamic-update-slice_fusion.8
  191.2 1.7 bitcast_dynamic-update-slice_fusion.7
  193.6 5.0 %gather_fusion = f32[16,4,128,128]{3,2,1,0:T(8,128)} fusion(f32[16,4,128,128]{3,2,1,0:T(8,128)} %bitcast.28, s32[1024]{0:T(1024)S(1)} %pad_clamp_fusion), kind=kCustom, calls=%fused_computation | custom fusion | bytes 8388672 | tf_op jit(solution)/shard_map/gather | solution.py:27
  198.6 4.3 %fusion.18 = (f32[16,1,128,128]{3,2,1,0:T(8,128)}, f32[16,128,128]{2,1,0:T(8,128)}, f32[16,128,128]{2,1,0:T(8,128)}, f32[16,128,128]{2,1,0:T(8,128)}) fusion(f32[16,4,128,128]{3,2,1,0:T(8,128)} %gather_fusion), kind=kLoop, calls=%fused_computation.91 | loop fusion | bytes 8388608 | tf_op jit(solution)/shard_map/slice | solution.py:103
  204.1 49.8 %while.70 = (s32[]{:T(128)}, f32[128,128]{1,0:T(8,128)S(1)}, f32[1,128,128]{2,1,0:T(8,128)S(1)}, f32[16,128,128]{2,1,0:T(8,128)}, f32[16,1,128,128]{3,2,1,0:T(8,...) while((s32[]{:T(128)}, f32[128,128]{1,0:T(8,128)S(1)}, ...), condition=%wide.region_5.6_spmd.clone, body=%wide.region_4.5_spmd.clone.sunk | while | flops 180227 | bytes 854135 | solution.py:61
  204.1 1.6 bitcast_dynamic-update-slice_fusion.32
  207.2 1.6 bitcast_dynamic-update-slice_fusion.32
  210.3 1.6 bitcast_dynamic-update-slice_fusion.32
  213.4 1.6 bitcast_dynamic-update-slice_fusion.32
  216.5 1.6 bitcast_dynamic-update-slice_fusion.32
  219.6 1.6 bitcast_dynamic-update-slice_fusion.32
  222.7 1.6 bitcast_dynamic-update-slice_fusion.32
  225.9 1.6 bitcast_dynamic-update-slice_fusion.32
  227.4 1.6 bitcast_dynamic-update-slice_fusion.31
  229.0 1.6 bitcast_dynamic-update-slice_fusion.32
  232.1 1.6 bitcast_dynamic-update-slice_fusion.32
  235.2 1.6 bitcast_dynamic-update-slice_fusion.32
  238.3 1.6 bitcast_dynamic-update-slice_fusion.32
  241.4 1.6 bitcast_dynamic-update-slice_fusion.32
  244.5 1.6 bitcast_dynamic-update-slice_fusion.32
  247.6 1.6 bitcast_dynamic-update-slice_fusion.32
  250.7 1.6 bitcast_dynamic-update-slice_fusion.32
  252.3 1.6 bitcast_dynamic-update-slice_fusion.31
  254.9 24.7 %while.71 = (s32[]{:T(128)}, f32[1,128,128]{2,1,0:T(8,128)S(1)}, f32[16,1,128,128]{3,2,1,0:T(8,128)}, f32[16,1,128,128]{3,2,1,0:T(8,128)}, f32[16,128,128]{2,1,0:T(8,128)}, /*index=5*/s32[]{:T(128)}, s32[]{:T(128)}, s32[]{:T(128)}) while((s32[]{:T(128)}, f32[1,128,128]{2,1,0:T(8,128)S(1)}, f32[16,1,128,128]{3,2,1,0:T(8,128)}, ...), condition=%wide.region_7.8_spmd.clone, body=%wide.region_6.7_spmd.clone.sunk | while | flops 49156 | bytes 327791 | solution.py:68
  280.5 1.9 collective-permute-start.18
  282.4 6.9 %collective-permute-done.18 = f32[128,128]{1,0:T(8,128)S(1)} collective-permute-done((f32[128,128]{1,0:T(8,128)S(1)}, f32[128,128]{1,0:T(8,128)S(1)}, u32[]{:S(2)}, u32[]{:S(2)}) %collective-permute-start.18) | collective-permute-done | bytes 65568 | tf_op jit(solution)/shard_map/ppermute | solution.py:47
  (168 shorter events, 125.0 us)
Async XLA Ops:
  0.0 13.4 %copy-start.3 = (f32[16,128,128]{2,1,0:T(8,128)S(1)}, f32[16,128,128]{2,1,0:T(8,128)}, u32[]{:S(2)}) copy-start(f32[16,128,128]{2,1,0:T(8,128)} %param.10) | copy-start | bytes 3145732
  1.0 12.4 %collective-permute-start = (f32[16,1,128]{2,1,0:T(1,128)S(1)}, f32[16,1,128]{2,1,0:T(1,128)S(1)}, u32[]{:S(2)}, u32[]{:S(2)}) collective-permute-start(f32[16,1,128]{2,1,0:T(1,128)S(1)} %get-tuple-element.500), channel_id=1, source_target_pairs={{0,1},{1,2},{2,3},{3,4},{4,5},{5,6},{6,7},{7,8},{8,9},{9,10},{10,1... | collective-permute-start | bytes 24584 | tf_op jit(solution)/shard_map/ppermute | solution.py:38
  2.9 10.5 %collective-permute-start.1 = (f32[16,1,128]{2,1,0:T(1,128)S(1)}, f32[16,1,128]{2,1,0:T(1,128)S(1)}, u32[]{:S(2)}, u32[]{:S(2)}) collective-permute-start(f32[16,1,128]{2,1,0:T(1,128)S(1)} %get-tuple-element.501), channel_id=1, source_target_pairs={{1,0},{2,1},{3,2},{4,3},{5,4},{6,5},{7,6},{8,7},{9,8},{10,9},{11,1... | collective-permute-start | bytes 24584 | tf_op jit(solution)/shard_map/ppermute | solution.py:39
  13.4 1.3 copy-start.1
  13.4 1.9 copy-start.2
  13.8 1.0 copy-start
  81.8 8.4 %collective-permute-start.2 = (f32[4,128,128]{2,1,0:T(8,128)S(1)}, f32[4,128,128]{2,1,0:T(8,128)}, u32[]{:S(2)}, u32[]{:S(2)}) collective-permute-start(f32[4,128,128]{2,1,0:T(8,128)S(1)} %pad_maximum_fusion.4), channel_id=1, source_target_pairs={{16,0},{32,16},{48,32},{64,48},{80,64},{96,80},{112,96},{128,112},... | collective-permute-start | bytes 786440 | tf_op jit(solution)/shard_map/ppermute | solution.py:47
  91.3 6.5 %collective-permute-start.3 = (f32[1,4,128,128]{3,2,1,0:T(8,128)S(1)}, f32[1,4,128,128]{3,2,1,0:T(8,128)S(1)}, u32[]{:S(2)}, u32[]{:S(2)}) collective-permute-start(f32[1,4,128,128]{3,2,1,0:T(8,128)S(1)} %fusion.10), channel_id=1, source_target_pairs={{0,16},{16,32},{32,48},{48,64},{64,80},{80,96},{96,112},{112,128},... | collective-permute-start | bytes 786440 | tf_op jit(solution)/shard_map/ppermute | solution.py:22
  97.7 0.7 copy-start.4
  98.4 8.8 %collective-permute-start.4 = (f32[1,4,128,128]{3,2,1,0:T(8,128)S(1)}, f32[1,4,128,128]{3,2,1,0:T(8,128)S(1)}, u32[]{:S(2)}, u32[]{:S(2)}) collective-permute-start(f32[1,4,128,128]{3,2,1,0:T(8,128)S(1)} %collective-permute-done.3), channel_id=1, source_target_pairs={{0,16},{16,32},{32,48},{48,64},{64,80},{80,96},{96,112},{112,128},... | collective-permute-start | bytes 786440 | tf_op jit(solution)/shard_map/ppermute | solution.py:22
  101.2 8.7 %collective-permute-start.11 = (f32[1,4,128,128]{3,2,1,0:T(8,128)S(1)}, f32[1,4,128,128]{3,2,1,0:T(8,128)S(1)}, u32[]{:S(2)}, u32[]{:S(2)}) collective-permute-start(f32[1,4,128,128]{3,2,1,0:T(8,128)S(1)} %fusion.10), channel_id=1, source_target_pairs={{16,0},{32,16},{48,32},{64,48},{80,64},{96,80},{112,96},{128,112},... | collective-permute-start | bytes 786440 | tf_op jit(solution)/shard_map/ppermute | solution.py:24
  107.2 12.3 %copy-start.7 = (f32[1,4,128,128]{3,2,1,0:T(8,128)}, f32[1,4,128,128]{3,2,1,0:T(8,128)S(1)}, u32[]{:S(2)}) copy-start(f32[1,4,128,128]{3,2,1,0:T(8,128)S(1)} %collective-permute-done.4) | copy-start | bytes 786436
  107.2 9.3 %collective-permute-start.5 = (f32[1,4,128,128]{3,2,1,0:T(8,128)S(1)}, f32[1,4,128,128]{3,2,1,0:T(8,128)S(1)}, u32[]{:S(2)}, u32[]{:S(2)}) collective-permute-start(f32[1,4,128,128]{3,2,1,0:T(8,128)S(1)} %collective-permute-done.4), channel_id=1, source_target_pairs={{0,16},{16,32},{32,48},{48,64},{64,80},{80,96},{96,112},{112,128},... | collective-permute-start | bytes 786440 | tf_op jit(solution)/shard_map/ppermute | solution.py:22
  110.0 0.7 copy-start.5
  110.7 8.8 %collective-permute-start.12 = (f32[1,4,128,128]{3,2,1,0:T(8,128)S(1)}, f32[1,4,128,128]{3,2,1,0:T(8,128)S(1)}, u32[]{:S(2)}, u32[]{:S(2)}) collective-permute-start(f32[1,4,128,128]{3,2,1,0:T(8,128)S(1)} %collective-permute-done.11), channel_id=1, source_target_pairs={{16,0},{32,16},{48,32},{64,48},{80,64},{96,80},{112,96},{128,112},... | collective-permute-start | bytes 786440 | tf_op jit(solution)/shard_map/ppermute | solution.py:24
  116.5 12.2 %copy-start.10 = (f32[1,4,128,128]{3,2,1,0:T(8,128)}, f32[1,4,128,128]{3,2,1,0:T(8,128)S(1)}, u32[]{:S(2)}) copy-start(f32[1,4,128,128]{3,2,1,0:T(8,128)S(1)} %collective-permute-done.5) | copy-start | bytes 786436
  116.5 10.8 %collective-permute-start.6 = (f32[1,4,128,128]{3,2,1,0:T(8,128)S(1)}, f32[1,4,128,128]{3,2,1,0:T(8,128)S(1)}, u32[]{:S(2)}, u32[]{:S(2)}) collective-permute-start(f32[1,4,128,128]{3,2,1,0:T(8,128)S(1)} %collective-permute-done.5), channel_id=1, source_target_pairs={{0,16},{16,32},{32,48},{48,64},{64,80},{80,96},{96,112},{112,128},... | collective-permute-start | bytes 786440 | tf_op jit(solution)/shard_map/ppermute | solution.py:22
  119.5 2.9 copy-start.8
  119.5 9.1 %collective-permute-start.13 = (f32[1,4,128,128]{3,2,1,0:T(8,128)S(1)}, f32[1,4,128,128]{3,2,1,0:T(8,128)S(1)}, u32[]{:S(2)}, u32[]{:S(2)}) collective-permute-start(f32[1,4,128,128]{3,2,1,0:T(8,128)S(1)} %collective-permute-done.12), channel_id=1, source_target_pairs={{16,0},{32,16},{48,32},{64,48},{80,64},{96,80},{112,96},{128,112},... | collective-permute-start | bytes 786440 | tf_op jit(solution)/shard_map/ppermute | solution.py:24
  127.3 25.0 %copy-start.15 = (f32[1,4,128,128]{3,2,1,0:T(8,128)}, f32[1,4,128,128]{3,2,1,0:T(8,128)S(1)}, u32[]{:S(2)}) copy-start(f32[1,4,128,128]{3,2,1,0:T(8,128)S(1)} %collective-permute-done.6) | copy-start | bytes 786436
  127.3 12.2 %collective-permute-start.7 = (f32[1,4,128,128]{3,2,1,0:T(8,128)S(1)}, f32[1,4,128,128]{3,2,1,0:T(8,128)S(1)}, u32[]{:S(2)}, u32[]{:S(2)}) collective-permute-start(f32[1,4,128,128]{3,2,1,0:T(8,128)S(1)} %collective-permute-done.6), channel_id=1, source_target_pairs={{0,16},{16,32},{32,48},{48,64},{64,80},{80,96},{96,112},{112,128},... | collective-permute-start | bytes 786440 | tf_op jit(solution)/shard_map/ppermute | solution.py:22
  128.6 5.1 %copy-start.11 = (f32[1,4,128,128]{3,2,1,0:T(8,128)}, f32[1,4,128,128]{3,2,1,0:T(8,128)S(1)}, u32[]{:S(2)}) copy-start(f32[1,4,128,128]{3,2,1,0:T(8,128)S(1)} %collective-permute-done.13) | copy-start | bytes 786436
  128.6 10.8 %collective-permute-start.14 = (f32[1,4,128,128]{3,2,1,0:T(8,128)S(1)}, f32[1,4,128,128]{3,2,1,0:T(8,128)S(1)}, u32[]{:S(2)}, u32[]{:S(2)}) collective-permute-start(f32[1,4,128,128]{3,2,1,0:T(8,128)S(1)} %collective-permute-done.13), channel_id=1, source_target_pairs={{16,0},{32,16},{48,32},{64,48},{80,64},{96,80},{112,96},{128,112},... | collective-permute-start | bytes 786440 | tf_op jit(solution)/shard_map/ppermute | solution.py:24
  139.4 18.4 %copy-start.16 = (f32[1,4,128,128]{3,2,1,0:T(8,128)}, f32[1,4,128,128]{3,2,1,0:T(8,128)S(1)}, u32[]{:S(2)}) copy-start(f32[1,4,128,128]{3,2,1,0:T(8,128)S(1)} %collective-permute-done.7) | copy-start | bytes 786436
  139.5 12.2 %collective-permute-start.8 = (f32[1,4,128,128]{3,2,1,0:T(8,128)S(1)}, f32[1,4,128,128]{3,2,1,0:T(8,128)S(1)}, u32[]{:S(2)}, u32[]{:S(2)}) collective-permute-start(f32[1,4,128,128]{3,2,1,0:T(8,128)S(1)} %collective-permute-done.7), channel_id=1, source_target_pairs={{0,16},{16,32},{32,48},{48,64},{64,80},{80,96},{96,112},{112,128},... | collective-permute-start | bytes 786440 | tf_op jit(solution)/shard_map/ppermute | solution.py:22
  139.5 0.7 copy-start.13
  140.2 12.1 %collective-permute-start.15 = (f32[1,4,128,128]{3,2,1,0:T(8,128)S(1)}, f32[1,4,128,128]{3,2,1,0:T(8,128)}, u32[]{:S(2)}, u32[]{:S(2)}) collective-permute-start(f32[1,4,128,128]{3,2,1,0:T(8,128)S(1)} %collective-permute-done.14), channel_id=1, source_target_pairs={{16,0},{32,16},{48,32},{64,48},{80,64},{96,80},{112,96},{128,112},... | collective-permute-start | bytes 786440 | tf_op jit(solution)/shard_map/ppermute | solution.py:24
  151.7 11.1 %copy-start.17 = (f32[1,4,128,128]{3,2,1,0:T(8,128)}, f32[1,4,128,128]{3,2,1,0:T(8,128)S(1)}, u32[]{:S(2)}) copy-start(f32[1,4,128,128]{3,2,1,0:T(8,128)S(1)} %collective-permute-done.8) | copy-start | bytes 786436
  151.7 11.1 %collective-permute-start.9 = (f32[1,4,128,128]{3,2,1,0:T(8,128)S(1)}, f32[1,4,128,128]{3,2,1,0:T(8,128)}, u32[]{:S(2)}, u32[]{:S(2)}) collective-permute-start(f32[1,4,128,128]{3,2,1,0:T(8,128)S(1)} %collective-permute-done.8), channel_id=1, source_target_pairs={{0,16},{16,32},{32,48},{48,64},{64,80},{80,96},{96,112},{112,128},... | collective-permute-start | bytes 786440 | tf_op jit(solution)/shard_map/ppermute | solution.py:22
  152.3 11.1 %collective-permute-start.16 = (f32[1,4,128,128]{3,2,1,0:T(8,128)}, f32[1,4,128,128]{3,2,1,0:T(8,128)}, u32[]{:S(2)}, u32[]{:S(2)}) collective-permute-start(f32[1,4,128,128]{3,2,1,0:T(8,128)} %collective-permute-done.15), channel_id=1, source_target_pairs={{16,0},{32,16},{48,32},{64,48},{80,64},{96,80},{112,96},{128,112},... | collective-permute-start | bytes 786440 | tf_op jit(solution)/shard_map/ppermute | solution.py:24
  162.8 9.7 %collective-permute-start.10 = (f32[1,4,128,128]{3,2,1,0:T(8,128)}, f32[1,4,128,128]{3,2,1,0:T(8,128)}, u32[]{:S(2)}, u32[]{:S(2)}) collective-permute-start(f32[1,4,128,128]{3,2,1,0:T(8,128)} %collective-permute-done.9), channel_id=1, source_target_pairs={{0,16},{16,32},{32,48},{48,64},{64,80},{80,96},{96,112},{112,128},... | collective-permute-start | bytes 786440 | tf_op jit(solution)/shard_map/ppermute | solution.py:22
  162.8 23.8 %copy-start.6 = (f32[1,4,128,128]{3,2,1,0:T(8,128)S(1)}, f32[1,4,128,128]{3,2,1,0:T(8,128)}, u32[]{:S(2)}) copy-start(f32[1,4,128,128]{3,2,1,0:T(8,128)} %copy-done.5) | copy-start | bytes 786436
  162.9 24.5 %copy-start.9 = (f32[1,4,128,128]{3,2,1,0:T(8,128)S(1)}, f32[1,4,128,128]{3,2,1,0:T(8,128)}, u32[]{:S(2)}) copy-start(f32[1,4,128,128]{3,2,1,0:T(8,128)} %copy-done.8) | copy-start | bytes 786436
  162.9 25.2 %copy-start.12 = (f32[1,4,128,128]{3,2,1,0:T(8,128)S(1)}, f32[1,4,128,128]{3,2,1,0:T(8,128)}, u32[]{:S(2)}) copy-start(f32[1,4,128,128]{3,2,1,0:T(8,128)} %copy-done.11) | copy-start | bytes 786436
  162.9 25.9 %copy-start.14 = (f32[1,4,128,128]{3,2,1,0:T(8,128)S(1)}, f32[1,4,128,128]{3,2,1,0:T(8,128)}, u32[]{:S(2)}) copy-start(f32[1,4,128,128]{3,2,1,0:T(8,128)} %copy-done.13) | copy-start | bytes 786436
  163.3 29.6 %collective-permute-start.17 = (f32[1,4,128,128]{3,2,1,0:T(8,128)}, f32[1,4,128,128]{3,2,1,0:T(8,128)S(1)}, u32[]{:S(2)}, u32[]{:S(2)}) collective-permute-start(f32[1,4,128,128]{3,2,1,0:T(8,128)} %collective-permute-done.16), channel_id=1, source_target_pairs={{16,0},{32,16},{48,32},{64,48},{80,64},{96,80},{112,96},{128,112},... | collective-permute-start | bytes 786440 | tf_op jit(solution)/shard_map/ppermute | solution.py:24
  280.5 8.9 %collective-permute-start.18 = (f32[128,128]{1,0:T(8,128)S(1)}, f32[128,128]{1,0:T(8,128)S(1)}, u32[]{:S(2)}, u32[]{:S(2)}) collective-permute-start(f32[128,128]{1,0:T(8,128)S(1)} %get-tuple-element.498), channel_id=1, source_target_pairs={{0,16},{16,32},{32,48},{48,64},{64,80},{80,96},{96,112},{112,128},... | collective-permute-start | bytes 196616 | tf_op jit(solution)/shard_map/ppermute | solution.py:47
